TPU v7x, 256 devices: a whole 4x4x8 slice. The times are simulated.
256 devices in a mesh: seq: 64 (over z, x, core), head: 4 (over y).
Axes of the slice: x: 4, y: 4, z: 8, core: 2. Of those that a mesh axis runs over, the one named last changes fastest.
Arguments:
- features: bfloat16 [8192, 4096], P('seq', 'head'), may hold values from -6 to 6
- proj_weight: bfloat16 [4096, 4096], P(None, 'head'), may hold values from -0.09375 to 0.09375
- query_vectors: bfloat16 [8192, 4096], P('seq', 'head'), may hold values from -6 to 6
- key_vectors: bfloat16 [8192, 4096], P('seq', 'head'), may hold values from -6 to 6
Outputs:
- rotated_queries: bfloat16 [8192, 4096], P('seq', 'head')
- rotated_keys: bfloat16 [8192, 4096], P('seq', 'head')
All inputs are finite; a program needn't handle non-finite values.
Results may differ from a plain program's by a relative error of at most 0.0024.
Values may be sent and summed in bfloat16 or wider, within the bound.
No kernel may reach another device: no remote copies, remote signals or barrier semaphores. Data moves between devices by JAX's collectives and lax.ppermute only.
A program may use at most 128 MiB of HBM per device.

v0:
```python
import functools
import jax
import jax.numpy as jnp
from jax import lax
from jax.sharding import PartitionSpec as P

HEAD_DIM = 128


def entering(array, axis, count, combine, identity):
    place = lax.axis_index(axis)
    start = jnp.broadcast_to(jnp.asarray(identity, array.dtype), array.shape)
    span = array
    before = None
    shift = 1
    while shift < count:
        pairs = [(k, k + shift) for k in range(count - shift)]
        arrived = lax.ppermute(span, axis, pairs)
        reached = place >= shift
        last = shift * 2 >= count
        if before is None:
            before = jnp.where(reached, arrived, start)
            if not last:
                span = jnp.where(reached, combine(arrived, span), span)
        elif last:
            before = jnp.where(reached, combine(arrived, before), before)
        else:
            width = array.shape[-1]
            both = combine(arrived, jnp.concatenate([span, before], axis=-1))
            span = jnp.where(reached, both[..., :width], span)
            before = jnp.where(reached, both[..., width:], before)
        shift = shift * 2
    return before if before is not None else start


def small_inverse(matrix):
    highest = lax.Precision.HIGHEST
    size = matrix.shape[-1]
    position = jnp.arange(size)
    strict = (position[:, None] < position[None, :]).astype(jnp.float32)
    eye_block = jnp.eye(size, dtype=jnp.float32)
    power = -2.0 * matrix * strict[None]
    result = eye_block[None] + power
    reach = 2
    while reach < size:
        power = jnp.einsum("hij,hjk->hik", power, power, precision=highest)
        result = result + jnp.einsum("hij,hjk->hik", result, power, precision=highest)
        reach = reach * 2
    return 2.0 * result


def triangle_inverse(matrix):
    highest = lax.Precision.HIGHEST
    size = matrix.shape[-1]
    if size <= 16:
        return small_inverse(matrix)
    half = size // 2
    first = triangle_inverse(matrix[:, :half, :half])
    second = triangle_inverse(matrix[:, half:, half:])
    coupling = matrix[:, :half, half:]
    middle = jnp.einsum("hij,hjk->hik", first, coupling, precision=highest)
    corner = -jnp.einsum("hij,hjk->hik", middle, second, precision=highest)
    lower_left = jnp.zeros((matrix.shape[0], size - half, half), jnp.float32)
    top = jnp.concatenate([first, corner], axis=2)
    bottom = jnp.concatenate([lower_left, second], axis=2)
    return jnp.concatenate([top, bottom], axis=1)


def upper_solve(matrix, right_side):
    highest = lax.Precision.HIGHEST
    rows = matrix.shape[1]
    size = min(128, rows)
    count = rows // size
    solved_blocks = []
    for i in reversed(range(count)):
        inverse_block = triangle_inverse(matrix)
        solved_blocks.append(
            jnp.einsum("hij,hjk->hik", inverse_block, right_side, precision=highest)
        )
    return jnp.concatenate(solved_blocks[::-1], axis=1)


def body(seq_count, features, proj_weight, query_vectors, key_vectors):
    highest = lax.Precision.HIGHEST
    tok_rows = query_vectors.shape[0]
    width = proj_weight.shape[1]
    local_heads = width // HEAD_DIM
    raw_proj = jnp.dot(
        lax.all_gather(features, "head", axis=1, tiled=True),
        proj_weight,
        preferred_element_type=jnp.float32,
    )
    raw_proj = raw_proj.reshape(tok_rows, local_heads, HEAD_DIM)
    directions = raw_proj * lax.rsqrt(jnp.sum(raw_proj * raw_proj, axis=-1, keepdims=True) + 1e-06)
    reflectors = jnp.transpose(directions, (1, 0, 2))
    targets = jnp.concatenate(
        [
            query_vectors.reshape(tok_rows, local_heads, HEAD_DIM),
            key_vectors.reshape(tok_rows, local_heads, HEAD_DIM),
        ],
        axis=0,
    )
    targets = jnp.transpose(targets.astype(jnp.float32), (1, 0, 2))
    gram = jnp.einsum("hid,hjd->hij", reflectors, reflectors, precision=highest)
    position = jnp.arange(tok_rows)
    upper = (position[:, None] < position[None, :]).astype(jnp.float32)
    identity_tok = jnp.eye(tok_rows, dtype=jnp.float32)
    inverse_t = gram * upper[None] + 0.5 * identity_tok[None]
    projected = jnp.einsum("hid,htd->hit", reflectors, targets, precision=highest)
    target_pos = jnp.concatenate([position, position])
    keep = (position[:, None] <= target_pos[None, :]).astype(jnp.float32)
    masked = projected * keep[None]
    right_side = jnp.concatenate([masked, reflectors], axis=2)
    solved = upper_solve(inverse_t, right_side)
    weights_tok = solved[:, :, : 2 * tok_rows]
    factor = solved[:, :, 2 * tok_rows :]
    local_part = targets - jnp.einsum("hit,hid->htd", weights_tok, reflectors, precision=highest)
    identity = jnp.broadcast_to(
        jnp.eye(HEAD_DIM, dtype=jnp.float32), (local_heads, HEAD_DIM, HEAD_DIM)
    )
    block_product = identity - jnp.einsum("hid,hie->hde", reflectors, factor, precision=highest)

    def combine(earlier, later):
        return jnp.einsum("hde,hef->hdf", earlier, later, precision=highest)

    carried = entering(block_product, "seq", seq_count, combine, identity)
    rotated = jnp.einsum("hde,hte->htd", carried, local_part, precision=highest)
    rotated = jnp.transpose(rotated, (1, 0, 2))
    rotated_queries = rotated[:tok_rows].reshape(tok_rows, width).astype(jnp.bfloat16)
    rotated_keys = rotated[tok_rows:].reshape(tok_rows, width).astype(jnp.bfloat16)
    return (rotated_queries, rotated_keys)


def solution(mesh):
    in_specs = (P("seq", "head"), P(None, "head"), P("seq", "head"), P("seq", "head"))
    out_specs = (P("seq", "head"), P("seq", "head"))
    return jax.shard_map(
        functools.partial(body, mesh.shape["seq"]),
        mesh=mesh,
        in_specs=in_specs,
        out_specs=out_specs,
        check_vma=False,
    )
```

profile of v0, /device:TPU:35, one launch (start us, length us, event | category | flops | bytes accessed | tf_op | source)
XLA Modules:
  0.0 207.6 jit_solution(11913831428166195170)
XLA Ops:
  7.2 0.7 all-gather.2.cloned.1.call-update
  7.9 1.1 copy.86
  9.2 1.1 copy.85
  10.8 26.2 %all-gather.2.cloned.1.call-done = bf16[128,4096]{1,0:T(8,128)(2,1)} async-done(((bf16[128,1024]{1,0:T(8,128)(2,1)}), bf16[128,4096]{1,0:T(8,128)(2,1)}) %all-gather.2.cloned.1.call-update) | async-done | bytes 1048592 | tf_op jit(solution)/shard_map/all_gather | solution.py:89
  37.0 5.0 %fusion.141 = f32[128,1024]{1,0:T(8,128)S(1)} fusion(bf16[128,4096]{1,0:T(8,128)(2,1)} %all-gather.2.cloned.1.call-done, bf16[4096,1024]{1,0:T(8,128)(2,1)} %param.5), kind=kOutput, calls=%fused_computation.212 | convolution fusion | flops 1073741824 | bytes 9961472 | tf_op jit(solution)/shard_map/dot_general | solution.py:88
  42.6 1.2 fusion.5
  43.8 0.3 fusion.102
  44.1 0.3 fusion.101
  45.3 0.3 fusion.100
  46.0 0.3 fusion.99
  46.3 0.3 convolution_add_fusion.11
  46.8 0.3 fusion.98
  47.0 0.3 convolution_add_fusion.14
  47.5 0.3 fusion.97
  48.2 0.3 fusion.96
  48.5 0.3 convolution_add_fusion.20
  53.0 0.3 fusion.61
  57.3 0.3 fusion.63
  57.9 0.5 fusion.47
  58.4 0.4 convolution_negate_fusion
  58.8 0.6 convolution_multiply_fusion
  59.5 1.7 fusion
  61.2 1.0 convolution_subtract_fusion.1
  62.2 5.7 %collective-permute-start = (f32[8,128,128]{1,2,0:T(8,128)S(1)}, f32[8,128,128]{1,2,0:T(8,128)S(1)}, u32[]{:S(2)}, u32[]{:S(2)}) collective-permute-start(f32[8,128,128]{1,2,0:T(8,128)S(1)} %convolution_subtract_fusion.1), channel_id=1, source_target_pairs={{0,4},{4,8},{8,12},{12,16},{16,20},{20,24},{24,28},{28,32},{32,36}... | collective-permute-start | bytes 1572872 | tf_op jit(solution)/shard_map/ppermute | solution.py:18
  68.0 6.1 %collective-permute-done = f32[8,128,128]{1,2,0:T(8,128)S(1)} collective-permute-done((f32[8,128,128]{1,2,0:T(8,128)S(1)}, f32[8,128,128]{1,2,0:T(8,128)S(1)}, u32[]{:S(2)}, u32[]{:S(2)}) %collective-permute-start) | collective-permute-done | bytes 524320 | tf_op jit(solution)/shard_map/ppermute | solution.py:18
  74.1 1.8 convolution_select_fusion.1
  75.9 2.8 %collective-permute-start.1 = (f32[8,128,128]{1,2,0:T(8,128)S(1)}, f32[8,128,128]{1,2,0:T(8,128)}, u32[]{:S(2)}, u32[]{:S(2)}) collective-permute-start(f32[8,128,128]{1,2,0:T(8,128)S(1)} %convolution_select_fusion.1), channel_id=1, source_target_pairs={{0,8},{4,12},{8,16},{12,20},{16,24},{20,28},{24,32},{28,36},{32,40... | collective-permute-start | bytes 1572872 | tf_op jit(solution)/shard_map/ppermute | solution.py:18
  78.7 10.6 %collective-permute-done.1 = f32[8,128,128]{1,2,0:T(8,128)} collective-permute-done((f32[8,128,128]{1,2,0:T(8,128)S(1)}, f32[8,128,128]{1,2,0:T(8,128)}, u32[]{:S(2)}, u32[]{:S(2)}) %collective-permute-start.1) | collective-permute-done | bytes 524320 | tf_op jit(solution)/shard_map/ppermute | solution.py:18
  89.3 2.0 fusion.15
  91.3 1.1 slice_select_fusion.7
  92.5 4.6 %collective-permute-start.2 = (f32[8,128,128]{1,2,0:T(8,128)}, f32[8,128,128]{1,2,0:T(8,128)S(1)}, u32[]{:S(2)}, u32[]{:S(2)}) collective-permute-start(f32[8,128,128]{1,2,0:T(8,128)} %get-tuple-element.15), channel_id=1, source_target_pairs={{0,16},{4,20},{8,24},{12,28},{16,32},{20,36},{24,40},{28,44},{32,4... | collective-permute-start | bytes 1572872 | tf_op jit(solution)/shard_map/ppermute | solution.py:18
  97.1 10.6 %collective-permute-done.2 = f32[8,128,128]{1,2,0:T(8,128)S(1)} collective-permute-done((f32[8,128,128]{1,2,0:T(8,128)}, f32[8,128,128]{1,2,0:T(8,128)S(1)}, u32[]{:S(2)}, u32[]{:S(2)}) %collective-permute-start.2) | collective-permute-done | bytes 524320 | tf_op jit(solution)/shard_map/ppermute | solution.py:18
  107.7 2.2 %fusion.19 = f32[8,128,256]{1,2,0:T(8,128)S(1)} fusion(f32[8,128,128]{1,2,0:T(8,128)S(1)} %collective-permute-done.2, f32[8,128,128]{1,2,0:T(8,128)} %get-tuple-element.14, f32[8,128,128]{1,2,0:T(8,128)} %get-tuple-element.15), kind=kOutput, calls=%fused_computation.57 | convolution fusion | flops 402915328 | bytes 2621440 | tf_op jit(solution)/shard_map/hde,hef->hdf/dot_general | solution.py:124
  109.9 0.9 slice_select_fusion.5
  110.8 3.2 %collective-permute-start.3 = (f32[8,128,128]{1,2,0:T(8,128)}, f32[8,128,128]{1,2,0:T(8,128)S(1)}, u32[]{:S(2)}, u32[]{:S(2)}) collective-permute-start(f32[8,128,128]{1,2,0:T(8,128)} %get-tuple-element.13), channel_id=1, source_target_pairs={{0,32},{4,36},{8,40},{12,44},{16,48},{20,52},{24,56},{28,60},{32,6... | collective-permute-start | bytes 1572872 | tf_op jit(solution)/shard_map/ppermute | solution.py:18
  114.0 8.6 %collective-permute-done.3 = f32[8,128,128]{1,2,0:T(8,128)S(1)} collective-permute-done((f32[8,128,128]{1,2,0:T(8,128)}, f32[8,128,128]{1,2,0:T(8,128)S(1)}, u32[]{:S(2)}, u32[]{:S(2)}) %collective-permute-start.3) | collective-permute-done | bytes 524320 | tf_op jit(solution)/shard_map/ppermute | solution.py:18
  122.6 2.0 fusion.23
  124.8 9.3 %collective-permute-start.4 = (f32[8,128,128]{1,2,0:T(8,128)S(1)}, f32[8,128,128]{1,2,0:T(8,128)}, u32[]{:S(2)}, u32[]{:S(2)}) collective-permute-start(f32[8,128,128]{1,2,0:T(8,128)S(1)} %get-tuple-element.11), channel_id=1, source_target_pairs={{0,64},{4,68},{8,72},{12,76},{16,80},{20,84},{24,88},{28,92},{32,9... | collective-permute-start | bytes 1572872 | tf_op jit(solution)/shard_map/ppermute | solution.py:18
  134.1 32.4 %collective-permute-done.4 = f32[8,128,128]{1,2,0:T(8,128)} collective-permute-done((f32[8,128,128]{1,2,0:T(8,128)S(1)}, f32[8,128,128]{1,2,0:T(8,128)}, u32[]{:S(2)}, u32[]{:S(2)}) %collective-permute-start.4) | collective-permute-done | bytes 524320 | tf_op jit(solution)/shard_map/ppermute | solution.py:18
  166.6 2.0 fusion.27
  168.6 1.0 slice_select_fusion.2
  169.8 6.0 %collective-permute-start.5 = (f32[8,128,128]{1,2,0:T(8,128)}, f32[8,128,128]{1,2,0:T(8,128)S(1)}, u32[]{:S(2)}, u32[]{:S(2)}) collective-permute-start(f32[8,128,128]{1,2,0:T(8,128)} %slice_select_fusion.2), channel_id=1, source_target_pairs={{0,128},{4,132},{8,136},{12,140},{16,144},{20,148},{24,152},{28,15... | collective-permute-start | bytes 1572872 | tf_op jit(solution)/shard_map/ppermute | solution.py:18
  175.8 3.0 %convolution_subtract_fusion = f32[8,256,128]{2,1,0:T(8,128)S(1)} fusion(f32[8,128,128]{2,1,0:T(8,128)S(1)} %fusion.31, f32[8,128,384]{2,1,0:T(8,128)S(1)} %fusion, bf16[128,8,128]{2,0,1:T(8,128)(2,1)S(1)} %copy.88, bf16[128,8,128]{2,0,1:T(8,128)(2,1)} %copy-done.4), kind=kOutput, calls=%fused_computation.4 | convolution fusion | flops 404226048 | bytes 3145728 | tf_op jit(solution)/shard_map/hit,hid->htd/dot_general | solution.py:117
  178.8 18.4 %collective-permute-done.5 = f32[8,128,128]{1,2,0:T(8,128)S(1)} collective-permute-done((f32[8,128,128]{1,2,0:T(8,128)}, f32[8,128,128]{1,2,0:T(8,128)S(1)}, u32[]{:S(2)}, u32[]{:S(2)}) %collective-permute-start.5) | collective-permute-done | bytes 524320 | tf_op jit(solution)/shard_map/ppermute | solution.py:18
  197.2 0.6 convolution_select_fusion
  197.8 1.1 fusion.4
  199.0 0.9 copy.115
  199.9 0.8 copy.116
  (86 shorter events, 11.9 us)
Async XLA Ops:
  7.2 29.8 %all-gather.2.cloned.1.call-start = ((), (), s32[]{:S(2)}) async-start(), calls=%async_computation | async-start | bytes 1310720 | tf_op jit(solution)/shard_map/all_gather | solution.py:89
  10.5 48.3 %copy-start.4 = (bf16[128,8,128]{2,0,1:T(8,128)(2,1)}, bf16[128,8,128]{2,0,1:T(8,128)(2,1)S(1)}, u32[]{:S(2)}) copy-start(bf16[128,8,128]{2,0,1:T(8,128)(2,1)S(1)} %copy.87) | copy-start | bytes 786436
  62.2 5.8 %copy-start.5 = (f32[8,128,128]{1,2,0:T(8,128)}, f32[8,128,128]{1,2,0:T(8,128)S(1)}, u32[]{:S(2)}) copy-start(f32[8,128,128]{1,2,0:T(8,128)S(1)} %convolution_subtract_fusion.1) | copy-start | bytes 1572868
  62.2 11.9 %collective-permute-start = (f32[8,128,128]{1,2,0:T(8,128)S(1)}, f32[8,128,128]{1,2,0:T(8,128)S(1)}, u32[]{:S(2)}, u32[]{:S(2)}) collective-permute-start(f32[8,128,128]{1,2,0:T(8,128)S(1)} %convolution_subtract_fusion.1), channel_id=1, source_target_pairs={{0,4},{4,8},{8,12},{12,16},{16,20},{20,24},{24,28},{28,32},{32,36}... | collective-permute-start | bytes 1572872 | tf_op jit(solution)/shard_map/ppermute | solution.py:18
  75.9 13.4 %collective-permute-start.1 = (f32[8,128,128]{1,2,0:T(8,128)S(1)}, f32[8,128,128]{1,2,0:T(8,128)}, u32[]{:S(2)}, u32[]{:S(2)}) collective-permute-start(f32[8,128,128]{1,2,0:T(8,128)S(1)} %convolution_select_fusion.1), channel_id=1, source_target_pairs={{0,8},{4,12},{8,16},{12,20},{16,24},{20,28},{24,32},{28,36},{32,40... | collective-permute-start | bytes 1572872 | tf_op jit(solution)/shard_map/ppermute | solution.py:18
  92.5 17.4 %copy-start = (f32[8,128,128]{1,2,0:T(8,128)S(1)}, f32[8,128,128]{1,2,0:T(8,128)}, u32[]{:S(2)}) copy-start(f32[8,128,128]{1,2,0:T(8,128)} %get-tuple-element.14) | copy-start | bytes 1572868
  92.5 15.2 %collective-permute-start.2 = (f32[8,128,128]{1,2,0:T(8,128)}, f32[8,128,128]{1,2,0:T(8,128)S(1)}, u32[]{:S(2)}, u32[]{:S(2)}) collective-permute-start(f32[8,128,128]{1,2,0:T(8,128)} %get-tuple-element.15), channel_id=1, source_target_pairs={{0,16},{4,20},{8,24},{12,28},{16,32},{20,36},{24,40},{28,44},{32,4... | collective-permute-start | bytes 1572872 | tf_op jit(solution)/shard_map/ppermute | solution.py:18
  110.8 11.8 %copy-start.1 = (f32[8,128,128]{1,2,0:T(8,128)}, f32[8,128,128]{1,2,0:T(8,128)S(1)}, u32[]{:S(2)}) copy-start(f32[8,128,128]{1,2,0:T(8,128)S(1)} %get-tuple-element.12) | copy-start | bytes 1572868
  110.8 11.8 %collective-permute-start.3 = (f32[8,128,128]{1,2,0:T(8,128)}, f32[8,128,128]{1,2,0:T(8,128)S(1)}, u32[]{:S(2)}, u32[]{:S(2)}) collective-permute-start(f32[8,128,128]{1,2,0:T(8,128)} %get-tuple-element.13), channel_id=1, source_target_pairs={{0,32},{4,36},{8,40},{12,44},{16,48},{20,52},{24,56},{28,60},{32,6... | collective-permute-start | bytes 1572872 | tf_op jit(solution)/shard_map/ppermute | solution.py:18
  124.8 41.8 %collective-permute-start.4 = (f32[8,128,128]{1,2,0:T(8,128)S(1)}, f32[8,128,128]{1,2,0:T(8,128)}, u32[]{:S(2)}, u32[]{:S(2)}) collective-permute-start(f32[8,128,128]{1,2,0:T(8,128)S(1)} %get-tuple-element.11), channel_id=1, source_target_pairs={{0,64},{4,68},{8,72},{12,76},{16,80},{20,84},{24,88},{28,92},{32,9... | collective-permute-start | bytes 1572872 | tf_op jit(solution)/shard_map/ppermute | solution.py:18
  168.6 1.2 copy-start.2
  169.8 27.4 %collective-permute-start.5 = (f32[8,128,128]{1,2,0:T(8,128)}, f32[8,128,128]{1,2,0:T(8,128)S(1)}, u32[]{:S(2)}, u32[]{:S(2)}) collective-permute-start(f32[8,128,128]{1,2,0:T(8,128)} %slice_select_fusion.2), channel_id=1, source_target_pairs={{0,128},{4,132},{8,136},{12,140},{16,144},{20,148},{24,152},{28,15... | collective-permute-start | bytes 1572872 | tf_op jit(solution)/shard_map/ppermute | solution.py:18
  175.8 21.4 %copy-start.3 = (f32[8,128,256]{1,2,0:T(8,128)S(1)}, f32[8,128,256]{1,2,0:T(8,128)}, u32[]{:S(2)}) copy-start(f32[8,128,256]{1,2,0:T(8,128)} %copy-done.2) | copy-start | bytes 3145732
Sparse Core Ops, SparseCore 0:
  9.8 27.1 all-gather.1
where the time goes:
time: 208 us
  waiting for transfers between devices  114 us (55%)
  matrix products  38.3 us (18%)
  starting transfers between devices  31.7 us (15%)
  between operations  14.8 us (7%)
  local copies, waits for them, and re-layouts  5.15 us (2%)
  other arithmetic  4.06 us (2%)
    ppermute x6, waiting for transfers between devices, entering(): arrived = lax.ppermute(span, axis, pairs)  86.6 us
    ppermute x6, starting transfers between devices, entering(): arrived = lax.ppermute(span, axis, pairs)  31.7 us
    all_gather x1, waiting for transfers between devices, body(): lax.all_gather(features, 'head', axis=1, tiled=True)  26.2 us
    dot_general x6, matrix products, combine(): return jnp.einsum('hde,hef->hdf', earlier, later, precision=highest)  10.7 us
    dot_general x24, matrix products, small_inverse(): power = jnp.einsum('hij,hjk->hik', power, power, precision=highest)  5.09 us
    dot_general x24, matrix products, small_inverse(): jnp.einsum('hij,hjk->hik', result, power, precision=highest)  5.05 us
    dot_general x1, matrix products, body(): jnp.dot(lax.all_gather(features, 'head', axis=1, tiled=True), proj_weight...  4.97 us
    unnamed x17, local copies, waits for them, and re-layouts  4.26 us
  transfers between devices with their start and end apart: 7, of which 7 were waited for; matrix products, arithmetic and copies ran while one was open for 3% of the time, Pallas kernels for 0%

commit v1 on v0

--- a/solution.py
+++ b/solution.py
@@ -85,10 +85,17 @@
     tok_rows = query_vectors.shape[0]
     width = proj_weight.shape[1]
     local_heads = width // HEAD_DIM
+
+    def joints_rest(on_dim, x_local):
+        return jnp.concatenate(
+            lax.all_to_all(
+                jnp.stack(tuple((x_local for _ in range(lax.axis_size("head")))), 0), "head", 0, 0
+            ),
+            axis=on_dim,
+        )
+
     raw_proj = jnp.dot(
-        lax.all_gather(features, "head", axis=1, tiled=True),
-        proj_weight,
-        preferred_element_type=jnp.float32,
+        joints_rest(1, x_local=features), proj_weight, preferred_element_type=jnp.float32
     )
     raw_proj = raw_proj.reshape(tok_rows, local_heads, HEAD_DIM)
     directions = raw_proj * lax.rsqrt(jnp.sum(raw_proj * raw_proj, axis=-1, keepdims=True) + 1e-06)

time: 208 us -> 190 us (0.913)
  waiting for transfers between devices: 114 us -> 86.7 us
  local copies, waits for them, and re-layouts: 5.15 us -> 18.7 us
  between operations: 14.8 us -> 1.47 us
  starting transfers between devices: 31.7 us -> 38.1 us
    all_gather x1 -> x0, waiting for transfers between devices: 26.2 us -> none  [body(): lax.all_gather(features, 'head', axis=1, tiled=True)]
    dot_general x0 -> x1, local copies, waits for them, and re-layouts: none -> 11.3 us  [body(): jnp.dot(joints_rest(1, x_local=features), proj_weight, preferred_element_...]
    all_to_all x0 -> x1, starting transfers between devices: none -> 4.18 us  [joints_rest(): lax.all_to_all(jnp.stack(tuple((x_local for _ in range(lax.axis_size('hea...]
    unnamed x17 -> x26, local copies, waits for them, and re-layouts: 4.26 us -> 1.98 us
    ppermute x6, starting transfers between devices: 31.7 us -> 33.9 us  [entering(): arrived = lax.ppermute(span, axis, pairs)]
    another operation x0 -> x1, local copies, waits for them, and re-layouts: none -> 2.17 us  [joints_rest(): jnp.stack(tuple((x_local for _ in range(lax.axis_size('head')))), 0)]
  transfers between devices with their start and end apart: 7 -> 7, of which waited for: 7 -> 7; matrix products, arithmetic and copies ran while one was open for 3% -> 8% of each run, Pallas kernels for 0% -> 0%
where the time goes in v1:
time: 190 us; the launch traced here: 189 us
  waiting for transfers between devices  86.7 us (46%)
  matrix products  39 us (21%)
  starting transfers between devices  38.1 us (20%)
  local copies, waits for them, and re-layouts  18.7 us (10%)
  other arithmetic  4.89 us (3%)
    ppermute x6, waiting for transfers between devices, entering(): arrived = lax.ppermute(span, axis, pairs)  85.4 us
    ppermute x6, starting transfers between devices, entering(): arrived = lax.ppermute(span, axis, pairs)  33.9 us
    dot_general x1, local copies, waits for them, and re-layouts, body(): jnp.dot(joints_rest(1, x_local=features), proj_weight, preferred_element_...  11.3 us
    dot_general x6, matrix products, combine(): return jnp.einsum('hde,hef->hdf', earlier, later, precision=highest)  10.8 us
    dot_general x1, matrix products, body(): jnp.dot(joints_rest(1, x_local=features), proj_weight, preferred_element_...  5.72 us
    dot_general x24, matrix products, small_inverse(): power = jnp.einsum('hij,hjk->hik', power, power, precision=highest)  5.09 us
    dot_general x24, matrix products, small_inverse(): jnp.einsum('hij,hjk->hik', result, power, precision=highest)  5.04 us
    all_to_all x1, starting transfers between devices, joints_rest(): lax.all_to_all(jnp.stack(tuple((x_local for _ in range(lax.axis_size('hea...  4.18 us
  transfers between devices with their start and end apart: 7, of which 7 were waited for; matrix products, arithmetic and copies ran while one was open for 8% of the time, Pallas kernels for 0%

profile of v1, /device:TPU:35, one launch (start us, length us, event | category | flops | bytes accessed | tf_op | source)
XLA Modules:
  0.0 188.8 jit_solution(4118693638022314917)
XLA Ops:
  0.6 2.2 %stack.2 = bf16[4,128,1024]{2,1,0:T(8,128)(2,1)} broadcast(bf16[128,1024]{1,0:T(8,128)(2,1)} %param.4), dimensions={1,2} | broadcast | bytes 1310720 | tf_op jit(solution)/shard_map/stack | solution.py:92
  2.8 4.2 %all-to-all-start = ((bf16[4,128,1024]{2,1,0:T(8,128)(2,1)}), bf16[4,128,1024]{2,1,0:T(8,128)(2,1)S(1)}, u32[]{:S(2)}, u32[]{:S(2)}) async-start(bf16[4,128,1024]{2,1,0:T(8,128)(2,1)} %stack.2), calls=%async_computation | async-start | bytes 2097152 | tf_op jit(solution)/shard_map/all_to_all | solution.py:91
  7.0 11.3 %copy.83 = bf16[1024,4096]{1,0:T(8,128)(2,1)} copy(bf16[1024,4096]{0,1:T(8,128)(2,1)} %bitcast.133) | data formatting | bytes 16777216 | tf_op jit(solution)/shard_map/dot_general | solution.py:97
  18.5 0.6 fusion.93
  19.1 0.7 fusion.74
  19.9 1.3 all-to-all-done
  21.2 0.8 copy.37
  22.1 0.8 reshape.99
  22.9 5.7 %multiply_reduce_fusion = (f32[128,8]{0,1:T(8,128)S(1)}, f32[128,8,128]{0,2,1:T(8,128)S(1)}) fusion(bf16[128,4096,1]{1,0,2:T(8,128)(2,1)S(1)} %reshape.99, bf16[8,128,4096]{2,1,0:T(8,128)(2,1)} %bitcast.132), kind=kOutput, calls=%fused_computation.94 | convolution fusion | flops 1074002944 | bytes 9965568 | tf_op jit(solution)/shard_map/dot_general | solution.py:97
  28.7 1.0 copy.41
  29.7 1.0 fusion.5
  30.7 0.3 fusion.101
  31.0 0.3 fusion.100
  32.9 0.3 fusion.98
  34.4 0.3 fusion.96
  35.2 0.3 fusion.95
  39.9 0.3 fusion.60
  44.2 0.3 fusion.62
  44.8 0.5 fusion.46
  45.4 0.4 convolution_negate_fusion
  45.8 0.7 convolution_multiply_fusion
  46.5 1.7 fusion
  48.2 1.0 convolution_subtract_fusion.1
  49.2 4.8 %collective-permute-start = (f32[8,128,128]{1,2,0:T(8,128)S(1)}, f32[8,128,128]{1,2,0:T(8,128)S(1)}, u32[]{:S(2)}, u32[]{:S(2)}) collective-permute-start(f32[8,128,128]{1,2,0:T(8,128)S(1)} %convolution_subtract_fusion.1), channel_id=1, source_target_pairs={{0,4},{4,8},{8,12},{12,16},{16,20},{20,24},{24,28},{28,32},{32,36}... | collective-permute-start | bytes 1572872 | tf_op jit(solution)/shard_map/ppermute | solution.py:18
  54.1 6.1 %collective-permute-done = f32[8,128,128]{1,2,0:T(8,128)S(1)} collective-permute-done((f32[8,128,128]{1,2,0:T(8,128)S(1)}, f32[8,128,128]{1,2,0:T(8,128)S(1)}, u32[]{:S(2)}, u32[]{:S(2)}) %collective-permute-start) | collective-permute-done | bytes 524320 | tf_op jit(solution)/shard_map/ppermute | solution.py:18
  60.2 1.9 convolution_select_fusion.1
  62.0 2.8 %collective-permute-start.1 = (f32[8,128,128]{1,2,0:T(8,128)S(1)}, f32[8,128,128]{1,2,0:T(8,128)}, u32[]{:S(2)}, u32[]{:S(2)}) collective-permute-start(f32[8,128,128]{1,2,0:T(8,128)S(1)} %convolution_select_fusion.1), channel_id=1, source_target_pairs={{0,8},{4,12},{8,16},{12,20},{16,24},{20,28},{24,32},{28,36},{32,40... | collective-permute-start | bytes 1572872 | tf_op jit(solution)/shard_map/ppermute | solution.py:18
  64.9 10.6 %collective-permute-done.1 = f32[8,128,128]{1,2,0:T(8,128)} collective-permute-done((f32[8,128,128]{1,2,0:T(8,128)S(1)}, f32[8,128,128]{1,2,0:T(8,128)}, u32[]{:S(2)}, u32[]{:S(2)}) %collective-permute-start.1) | collective-permute-done | bytes 524320 | tf_op jit(solution)/shard_map/ppermute | solution.py:18
  75.5 2.0 %fusion.15 = f32[8,128,256]{1,2,0:T(8,128)S(1)} fusion(f32[8,128,128]{1,2,0:T(8,128)} %collective-permute-done.1, f32[8,128,128]{1,2,0:T(8,128)S(1)} %broadcast_select_fusion, f32[8,128,128]{1,2,0:T(8,128)S(1)} %convolution_select_fusion.1), kind=kOutput, calls=%fused_computation.53 | convolution fusion | flops 402915328 | bytes 2621440 | tf_op jit(solution)/shard_map/hde,hef->hdf/dot_general | solution.py:131
  77.5 1.1 slice_select_fusion.7
  78.7 5.2 %collective-permute-start.2 = (f32[8,128,128]{1,2,0:T(8,128)}, f32[8,128,128]{1,2,0:T(8,128)S(1)}, u32[]{:S(2)}, u32[]{:S(2)}) collective-permute-start(f32[8,128,128]{1,2,0:T(8,128)} %get-tuple-element.11), channel_id=1, source_target_pairs={{0,16},{4,20},{8,24},{12,28},{16,32},{20,36},{24,40},{28,44},{32,4... | collective-permute-start | bytes 1572872 | tf_op jit(solution)/shard_map/ppermute | solution.py:18
  83.9 10.0 %collective-permute-done.2 = f32[8,128,128]{1,2,0:T(8,128)S(1)} collective-permute-done((f32[8,128,128]{1,2,0:T(8,128)}, f32[8,128,128]{1,2,0:T(8,128)S(1)}, u32[]{:S(2)}, u32[]{:S(2)}) %collective-permute-start.2) | collective-permute-done | bytes 524320 | tf_op jit(solution)/shard_map/ppermute | solution.py:18
  93.9 2.2 %fusion.19 = f32[8,128,256]{1,2,0:T(8,128)S(1)} fusion(f32[8,128,128]{1,2,0:T(8,128)S(1)} %collective-permute-done.2, f32[8,128,128]{1,2,0:T(8,128)} %get-tuple-element.10, f32[8,128,128]{1,2,0:T(8,128)} %get-tuple-element.11), kind=kOutput, calls=%fused_computation.57 | convolution fusion | flops 402915328 | bytes 2621440 | tf_op jit(solution)/shard_map/hde,hef->hdf/dot_general | solution.py:131
  96.1 0.9 slice_select_fusion.5
  97.0 3.5 %collective-permute-start.3 = (f32[8,128,128]{1,2,0:T(8,128)}, f32[8,128,128]{1,2,0:T(8,128)S(1)}, u32[]{:S(2)}, u32[]{:S(2)}) collective-permute-start(f32[8,128,128]{1,2,0:T(8,128)} %get-tuple-element.9), channel_id=1, source_target_pairs={{0,32},{4,36},{8,40},{12,44},{16,48},{20,52},{24,56},{28,60},{32,6... | collective-permute-start | bytes 1572872 | tf_op jit(solution)/shard_map/ppermute | solution.py:18
  100.6 8.3 %collective-permute-done.3 = f32[8,128,128]{1,2,0:T(8,128)S(1)} collective-permute-done((f32[8,128,128]{1,2,0:T(8,128)}, f32[8,128,128]{1,2,0:T(8,128)S(1)}, u32[]{:S(2)}, u32[]{:S(2)}) %collective-permute-start.3) | collective-permute-done | bytes 524320 | tf_op jit(solution)/shard_map/ppermute | solution.py:18
  108.9 2.0 %fusion.23 = f32[8,128,256]{1,2,0:T(8,128)S(1)} fusion(f32[8,128,128]{1,2,0:T(8,128)S(1)} %collective-permute-done.3, f32[8,128,128]{1,2,0:T(8,128)S(1)} %get-tuple-element.8, f32[8,128,128]{1,2,0:T(8,128)} %get-tuple-element.9), kind=kOutput, calls=%fused_computation.61 | convolution fusion | flops 402915328 | bytes 2621440 | tf_op jit(solution)/shard_map/hde,hef->hdf/dot_general | solution.py:131
  111.1 11.2 %collective-permute-start.4 = (f32[8,128,128]{1,2,0:T(8,128)S(1)}, f32[8,128,128]{1,2,0:T(8,128)}, u32[]{:S(2)}, u32[]{:S(2)}) collective-permute-start(f32[8,128,128]{1,2,0:T(8,128)S(1)} %get-tuple-element.7), channel_id=1, source_target_pairs={{0,64},{4,68},{8,72},{12,76},{16,80},{20,84},{24,88},{28,92},{32,9... | collective-permute-start | bytes 1572872 | tf_op jit(solution)/shard_map/ppermute | solution.py:18
  122.2 32.4 %collective-permute-done.4 = f32[8,128,128]{1,2,0:T(8,128)} collective-permute-done((f32[8,128,128]{1,2,0:T(8,128)S(1)}, f32[8,128,128]{1,2,0:T(8,128)}, u32[]{:S(2)}, u32[]{:S(2)}) %collective-permute-start.4) | collective-permute-done | bytes 524320 | tf_op jit(solution)/shard_map/ppermute | solution.py:18
  154.7 2.0 %fusion.27 = f32[8,128,256]{1,2,0:T(8,128)S(1)} fusion(f32[8,128,128]{1,2,0:T(8,128)} %collective-permute-done.4, f32[8,128,128]{1,2,0:T(8,128)S(1)} %get-tuple-element.6, f32[8,128,128]{1,2,0:T(8,128)S(1)} %get-tuple-element.7), kind=kOutput, calls=%fused_computation.65 | convolution fusion | flops 402915328 | bytes 2621440 | tf_op jit(solution)/shard_map/hde,hef->hdf/dot_general | solution.py:131
  156.7 0.9 slice_select_fusion.2
  157.9 6.3 %collective-permute-start.5 = (f32[8,128,128]{1,2,0:T(8,128)}, f32[8,128,128]{1,2,0:T(8,128)S(1)}, u32[]{:S(2)}, u32[]{:S(2)}) collective-permute-start(f32[8,128,128]{1,2,0:T(8,128)} %slice_select_fusion.2), channel_id=1, source_target_pairs={{0,128},{4,132},{8,136},{12,140},{16,144},{20,148},{24,152},{28,15... | collective-permute-start | bytes 1572872 | tf_op jit(solution)/shard_map/ppermute | solution.py:18
  164.2 3.1 %convolution_subtract_fusion = f32[8,256,128]{2,1,0:T(8,128)S(1)} fusion(f32[8,128,128]{1,2,0:T(8,128)S(1)} %bitcast_multiply_fusion, f32[8,128,384]{2,1,0:T(8,128)S(1)} %fusion, bf16[128,8,128]{2,0,1:T(8,128)(2,1)} %copy-done.5, bf16[128,8,128]{2,0,1:T(8,128)(2,1)} %copy-done.6), kind=kOutput, calls=%fused_computation.4 | convolution fusion | flops 404226048 | bytes 3145728 | tf_op jit(solution)/shard_map/hit,hid->htd/dot_general | solution.py:124
  167.3 18.0 %collective-permute-done.5 = f32[8,128,128]{1,2,0:T(8,128)S(1)} collective-permute-done((f32[8,128,128]{1,2,0:T(8,128)}, f32[8,128,128]{1,2,0:T(8,128)S(1)}, u32[]{:S(2)}, u32[]{:S(2)}) %collective-permute-start.5) | collective-permute-done | bytes 524320 | tf_op jit(solution)/shard_map/ppermute | solution.py:18
  185.2 0.6 convolution_select_fusion
  185.9 1.1 fusion.4
  187.1 0.9 copy.63
  188.0 0.8 copy.64
  (96 shorter events, 12.5 us)
Async XLA Ops:
  0.6 19.1 %copy-start = (bf16[128,1024]{1,0:T(8,128)(2,1)S(1)}, bf16[128,1024]{1,0:T(8,128)(2,1)}, u32[]{:S(2)}) copy-start(bf16[128,1024]{1,0:T(8,128)(2,1)} %param.6) | copy-start | bytes 786436
  2.8 18.4 %all-to-all-start = ((bf16[4,128,1024]{2,1,0:T(8,128)(2,1)}), bf16[4,128,1024]{2,1,0:T(8,128)(2,1)S(1)}, u32[]{:S(2)}, u32[]{:S(2)}) async-start(bf16[4,128,1024]{2,1,0:T(8,128)(2,1)} %stack.2), calls=%async_computation | async-start | bytes 2097152 | tf_op jit(solution)/shard_map/all_to_all | solution.py:91
  7.0 12.7 %copy-start.10 = (bf16[128,1024]{1,0:T(8,128)(2,1)S(1)}, bf16[128,1024]{1,0:T(8,128)(2,1)}, u32[]{:S(2)}) copy-start(bf16[128,1024]{1,0:T(8,128)(2,1)} %param.7) | copy-start | bytes 786436
  19.9 25.9 %copy-start.5 = (bf16[128,8,128]{2,0,1:T(8,128)(2,1)}, bf16[128,8,128]{2,0,1:T(8,128)(2,1)S(1)}, u32[]{:S(2)}) copy-start(bf16[128,8,128]{2,0,1:T(8,128)(2,1)S(1)} %get-tuple-element.16) | copy-start | bytes 786436
  19.9 25.9 %copy-start.6 = (bf16[128,8,128]{2,0,1:T(8,128)(2,1)}, bf16[128,8,128]{2,0,1:T(8,128)(2,1)S(1)}, u32[]{:S(2)}) copy-start(bf16[128,8,128]{2,0,1:T(8,128)(2,1)S(1)} %get-tuple-element.17) | copy-start | bytes 786436
  28.6 1.1 copy-start.11
  43.6 2.2 %copy-start.9 = (f32[128,256]{1,0:T(8,128)S(1)}, f32[128,256]{1,0:T(8,128)}, u32[]{:S(2)}) copy-start(f32[128,256]{1,0:T(8,128)} %fusion.74) | copy-start | bytes 393220
  45.4 1.1 copy-start.8
  49.2 4.8 %copy-start.7 = (f32[8,128,128]{1,2,0:T(8,128)}, f32[8,128,128]{1,2,0:T(8,128)S(1)}, u32[]{:S(2)}) copy-start(f32[8,128,128]{1,2,0:T(8,128)S(1)} %convolution_subtract_fusion.1) | copy-start | bytes 1572868
  49.2 10.9 %collective-permute-start = (f32[8,128,128]{1,2,0:T(8,128)S(1)}, f32[8,128,128]{1,2,0:T(8,128)S(1)}, u32[]{:S(2)}, u32[]{:S(2)}) collective-permute-start(f32[8,128,128]{1,2,0:T(8,128)S(1)} %convolution_subtract_fusion.1), channel_id=1, source_target_pairs={{0,4},{4,8},{8,12},{12,16},{16,20},{20,24},{24,28},{28,32},{32,36}... | collective-permute-start | bytes 1572872 | tf_op jit(solution)/shard_map/ppermute | solution.py:18
  62.0 13.5 %collective-permute-start.1 = (f32[8,128,128]{1,2,0:T(8,128)S(1)}, f32[8,128,128]{1,2,0:T(8,128)}, u32[]{:S(2)}, u32[]{:S(2)}) collective-permute-start(f32[8,128,128]{1,2,0:T(8,128)S(1)} %convolution_select_fusion.1), channel_id=1, source_target_pairs={{0,8},{4,12},{8,16},{12,20},{16,24},{20,28},{24,32},{28,36},{32,40... | collective-permute-start | bytes 1572872 | tf_op jit(solution)/shard_map/ppermute | solution.py:18
  78.7 17.4 %copy-start.1 = (f32[8,128,128]{1,2,0:T(8,128)S(1)}, f32[8,128,128]{1,2,0:T(8,128)}, u32[]{:S(2)}) copy-start(f32[8,128,128]{1,2,0:T(8,128)} %get-tuple-element.10) | copy-start | bytes 1572868
  78.7 15.2 %collective-permute-start.2 = (f32[8,128,128]{1,2,0:T(8,128)}, f32[8,128,128]{1,2,0:T(8,128)S(1)}, u32[]{:S(2)}, u32[]{:S(2)}) collective-permute-start(f32[8,128,128]{1,2,0:T(8,128)} %get-tuple-element.11), channel_id=1, source_target_pairs={{0,16},{4,20},{8,24},{12,28},{16,32},{20,36},{24,40},{28,44},{32,4... | collective-permute-start | bytes 1572872 | tf_op jit(solution)/shard_map/ppermute | solution.py:18
  97.0 11.8 %copy-start.2 = (f32[8,128,128]{1,2,0:T(8,128)}, f32[8,128,128]{1,2,0:T(8,128)S(1)}, u32[]{:S(2)}) copy-start(f32[8,128,128]{1,2,0:T(8,128)S(1)} %get-tuple-element.8) | copy-start | bytes 1572868
  97.0 11.8 %collective-permute-start.3 = (f32[8,128,128]{1,2,0:T(8,128)}, f32[8,128,128]{1,2,0:T(8,128)S(1)}, u32[]{:S(2)}, u32[]{:S(2)}) collective-permute-start(f32[8,128,128]{1,2,0:T(8,128)} %get-tuple-element.9), channel_id=1, source_target_pairs={{0,32},{4,36},{8,40},{12,44},{16,48},{20,52},{24,56},{28,60},{32,6... | collective-permute-start | bytes 1572872 | tf_op jit(solution)/shard_map/ppermute | solution.py:18
  111.1 43.6 %collective-permute-start.4 = (f32[8,128,128]{1,2,0:T(8,128)S(1)}, f32[8,128,128]{1,2,0:T(8,128)}, u32[]{:S(2)}, u32[]{:S(2)}) collective-permute-start(f32[8,128,128]{1,2,0:T(8,128)S(1)} %get-tuple-element.7), channel_id=1, source_target_pairs={{0,64},{4,68},{8,72},{12,76},{16,80},{20,84},{24,88},{28,92},{32,9... | collective-permute-start | bytes 1572872 | tf_op jit(solution)/shard_map/ppermute | solution.py:18
  156.7 1.2 copy-start.3
  157.9 27.4 %collective-permute-start.5 = (f32[8,128,128]{1,2,0:T(8,128)}, f32[8,128,128]{1,2,0:T(8,128)S(1)}, u32[]{:S(2)}, u32[]{:S(2)}) collective-permute-start(f32[8,128,128]{1,2,0:T(8,128)} %slice_select_fusion.2), channel_id=1, source_target_pairs={{0,128},{4,132},{8,136},{12,140},{16,144},{20,148},{24,152},{28,15... | collective-permute-start | bytes 1572872 | tf_op jit(solution)/shard_map/ppermute | solution.py:18
  164.2 21.0 %copy-start.4 = (f32[8,128,256]{1,2,0:T(8,128)S(1)}, f32[8,128,256]{1,2,0:T(8,128)}, u32[]{:S(2)}) copy-start(f32[8,128,256]{1,2,0:T(8,128)} %copy-done.3) | copy-start | bytes 3145732
